TPU v7x, 256 devices: a whole 4x4x8 slice. The times are simulated.
256 devices in a mesh: tm: 64 (over y, z, core), state: 4 (over x).
Axes of the slice: x: 4, y: 4, z: 8, core: 2. Of those that a mesh axis runs over, the one named last changes fastest.
Arguments:
- dynamics: float32 [512, 512], P('state'), may hold values from -1 to 1
- pattern: int32 [4, 4], replicated, may hold values from 0 to 1
- initial_mean: float32 [4, 512], replicated, may hold values from -6 to 6
- observed: float32 [1024, 4], P('tm'), may hold values from -6 to 6
- obs_index: int32 [1024], P('tm'), may hold values from 0 to 511
- obs_noise: float32 [1024], P('tm'), may hold values from 0.5 to 4
Outputs:
- filtered: float32 [1024, 4, 512], P('tm', 'state')
- smoothed: float32 [1024, 4, 512], P('tm', 'state')
All inputs are finite; a program needn't handle non-finite values.
Results may differ from a plain program's by a relative error of at most 0.0003.
Values sent between devices are 32-bit elements; how exact they have to be, the bound alone decides.
No kernel may reach another device: no remote copies, remote signals or barrier semaphores. Data moves between devices by JAX's collectives and lax.ppermute only.
A program may use at most 256 MiB of HBM per device.

v0:
```python
import jax
import jax.numpy as jnp
from jax import lax
from jax.sharding import PartitionSpec as P

AXES = ("tm", "state")


def product(left, right):
    return jnp.dot(left, right, precision=lax.Precision.HIGHEST, preferred_element_type=jnp.float32)


def transposed(left, right):
    return lax.dot_general(
        left,
        right,
        (((1,), (1,)), ((), ())),
        precision=lax.Precision.HIGHEST,
        preferred_element_type=jnp.float32,
    )


def leading(left, right):
    return lax.dot_general(
        left,
        right,
        (((0,), (0,)), ((), ())),
        precision=lax.Precision.HIGHEST,
        preferred_element_type=jnp.float32,
    )


def shifted(block, distance, total):
    route = [(i, i + distance) for i in range(total) if 0 <= i + distance < total]
    return lax.ppermute(block, AXES, route)


def per_device(dynamics, pattern, initial_mean, observed, obs_index, obs_noise):
    state_width = dynamics.shape[1]
    blocks = pattern.shape[0]
    block_span = state_width // blocks
    seq_total = initial_mean.shape[0]
    members = lax.axis_size("state")
    segments = lax.axis_size("tm") * members
    member = lax.axis_index("state")
    segment = lax.axis_index(AXES)
    span = observed.shape[0] // members
    steps_total = span * segments
    present = jnp.maximum(pattern, jnp.eye(blocks, dtype=jnp.int32))
    block_mask = jnp.repeat(jnp.repeat(present, block_span, 0), block_span, 1).astype(jnp.float32)
    transition = lax.all_gather(dynamics, "state", axis=0, tiled=True) * block_mask
    first = member * span
    obs_here = lax.dynamic_slice_in_dim(observed, first, span, 0)
    index_here = lax.dynamic_slice_in_dim(obs_index, first, span, 0)
    noise_here = lax.dynamic_slice_in_dim(obs_noise, first, span, 0)
    gains = 1.0 / (1.0 + noise_here)
    state_index = jnp.arange(state_width, dtype=jnp.int32)
    hits = (state_index[None, :] == index_here[:, None]).astype(jnp.float32)
    scales = 1.0 - gains[:, None] * hits
    global_step = segment * span + jnp.arange(span, dtype=jnp.int32)
    keeps = jnp.where(global_step == steps_total - 1, 0.0, 1.0).astype(jnp.float32)
    pushes = [(gains[j] * obs_here[j])[:, None] * hits[j][None, :] for j in range(span)]
    filt_a = transition * scales[0][:, None]
    filt_b = pushes[0]
    for j in range(1, span):
        filt_a = product(transition, filt_a) * scales[j][:, None]
        filt_b = transposed(filt_b, transition) * scales[j][None, :] + pushes[j]
    last = span - 1
    smooth_q = keeps[last] * (transition.T * scales[last][:, None])
    for j in range(last - 1, -1, -1):
        smooth_q = keeps[j] * (leading(transition, smooth_q) * scales[j][:, None])
    levels = 0
    while 2 ** (levels + 1) < segments:
        levels += 1
    stored_q = []
    for level in range(levels):
        distance = 2**level
        arrived_a, arrived_b = shifted((filt_a, filt_b), distance, segments)
        arrived_q = shifted(smooth_q, -distance, segments)
        usable = segment >= distance
        new_a = product(filt_a, arrived_a)
        new_b = transposed(arrived_b, filt_a) + filt_b
        filt_a = jnp.where(usable, new_a, filt_a)
        filt_b = jnp.where(usable, new_b, filt_b)
        stored_q.append(smooth_q)
        smooth_q = jnp.where(segment + distance < segments, product(smooth_q, arrived_q), smooth_q)
    stored_q.append(smooth_q)
    top = 2**levels
    prefix = transposed(initial_mean, filt_a) + filt_b
    if top < segments:
        arrived = shifted(prefix, top, segments)
        prefix = jnp.where(segment >= top, transposed(arrived, filt_a) + filt_b, prefix)
    entry = jnp.where(segment == 0, initial_mean, shifted(prefix, 1, segments))
    filtered = []
    current = entry
    for j in range(span):
        current = transposed(current, transition) * scales[j][None, :] + pushes[j]
        filtered.append(current)
    filtered = jnp.stack(filtered)
    mapped = product(
        transposed(filtered.reshape(span * seq_total, state_width), transition), transition
    ).reshape(span, seq_total, state_width)
    gaps = filtered - keeps[:, None, None] * mapped * scales[:, None, :]
    offsets = jnp.zeros((seq_total, state_width), jnp.float32)
    for j in range(last, -1, -1):
        offsets = keeps[j] * product(offsets, transition) * scales[j][None, :] + gaps[j]
    for level in range(levels):
        distance = 2**level
        arrived = shifted(offsets, -distance, segments)
        offsets = jnp.where(
            segment + distance < segments, transposed(arrived, stored_q[level]) + offsets, offsets
        )
    if top < segments:
        arrived = shifted(offsets, -top, segments)
        offsets = jnp.where(
            segment + top < segments, transposed(arrived, stored_q[levels]) + offsets, offsets
        )
    current = shifted(offsets, -1, segments)
    smoothed = [None] * span
    for j in range(last, -1, -1):
        current = keeps[j] * product(current, transition) * scales[j][None, :] + gaps[j]
        smoothed[j] = current
    smoothed = jnp.stack(smoothed)
    both = jnp.stack([filtered, smoothed])
    both = lax.all_to_all(both, "state", split_axis=2, concat_axis=1, tiled=True)
    return (both[0], both[1])


def solution(mesh):
    return jax.shard_map(
        per_device,
        mesh=mesh,
        in_specs=(P("state", None), P(), P(), P("tm", None), P("tm"), P("tm")),
        out_specs=(P("tm", "state", None), P("tm", "state", None)),
        check_vma=False,
    )
```

profile of v0, /device:TPU:232, one launch (start us, length us, event | category | flops | bytes accessed | tf_op | source)
XLA Modules:
  0.0 522.6 jit_solution(9289157682158466495)
XLA Ops:
  9.4 27.4 %all-gather.2.cloned.1.call-done = f32[512,512]{1,0:T(8,128)} async-done(((f32[128,512]{1,0:T(8,128)}), f32[512,512]{1,0:T(8,128)}) %all-gather.2.cloned.1.call-update) | async-done | bytes 1048592 | tf_op jit(solution)/shard_map/all_gather | solution.py:51
  43.9 2.2 collective-permute-start
  46.2 20.8 %collective-permute-done = f32[512,512]{1,0:T(8,128)} collective-permute-done((f32[512,512]{1,0:T(8,128)S(1)}, f32[512,512]{1,0:T(8,128)}, u32[]{:S(2)}, u32[]{:S(2)}) %collective-permute-start) | collective-permute-done | bytes 1048608 | tf_op jit(solution)/shard_map/ppermute | solution.py:35
  67.0 3.1 convolution_select_fusion.13
  70.1 6.3 %collective-permute-start.1 = (f32[512,512]{1,0:T(8,128)S(1)}, f32[512,512]{1,0:T(8,128)}, u32[]{:S(2)}, u32[]{:S(2)}) collective-permute-start(f32[512,512]{1,0:T(8,128)S(1)} %convolution_select_fusion.13), channel_id=1, source_target_pairs={{0,2},{1,3},{2,4},{3,5},{4,6},{5,7},{6,8},{7,9},{8,10},{9,11},{10,... | collective-permute-start | bytes 3145736 | tf_op jit(solution)/shard_map/ppermute | solution.py:35
  77.1 22.1 %collective-permute-done.1 = f32[512,512]{1,0:T(8,128)} collective-permute-done((f32[512,512]{1,0:T(8,128)S(1)}, f32[512,512]{1,0:T(8,128)}, u32[]{:S(2)}, u32[]{:S(2)}) %collective-permute-start.1) | collective-permute-done | bytes 1048608 | tf_op jit(solution)/shard_map/ppermute | solution.py:35
  99.2 3.1 convolution_select_fusion.12
  102.3 2.7 collective-permute-start.2
  105.0 4.9 fusion.7
  109.9 2.5 fusion.6
  112.4 2.6 fusion.5
  115.0 3.1 collective-permute-start.18
  118.9 2.9 convolution_select_fusion.11
  121.8 4.9 collective-permute-start.3
  126.6 2.8 multiply_reduce_fusion
  129.5 13.0 %collective-permute-done.18 = f32[512,512]{1,0:T(8,128)} collective-permute-done((f32[512,512]{1,0:T(8,128)S(1)}, f32[512,512]{1,0:T(8,128)}, u32[]{:S(2)}, u32[]{:S(2)}) %collective-permute-start.18) | collective-permute-done | bytes 1048608 | tf_op jit(solution)/shard_map/ppermute | solution.py:35
  142.4 3.1 convolution_select_fusion.6
  145.5 6.5 %collective-permute-start.20 = (f32[512,512]{1,0:T(8,128)S(1)}, f32[512,512]{1,0:T(8,128)S(1)}, u32[]{:S(2)}, u32[]{:S(2)}) collective-permute-start(f32[512,512]{1,0:T(8,128)S(1)} %convolution_select_fusion.6), channel_id=1, source_target_pairs={{2,0},{3,1},{4,2},{5,3},{6,4},{7,5},{8,6},{9,7},{10,8},{11,9},{12,... | collective-permute-start | bytes 3145736 | tf_op jit(solution)/shard_map/ppermute | solution.py:35
  153.0 3.7 convolution_select_fusion.10
  156.8 3.3 collective-permute-start.4
  164.1 11.0 %collective-permute-done.20 = f32[512,512]{1,0:T(8,128)S(1)} collective-permute-done((f32[512,512]{1,0:T(8,128)S(1)}, f32[512,512]{1,0:T(8,128)S(1)}, u32[]{:S(2)}, u32[]{:S(2)}) %collective-permute-start.20) | collective-permute-done | bytes 1048608 | tf_op jit(solution)/shard_map/ppermute | solution.py:35
  175.1 2.9 convolution_select_fusion.5
  177.9 2.4 collective-permute-start.22
  180.3 21.0 %collective-permute-done.7 = f32[4,512]{1,0:T(4,128)S(1)} collective-permute-done((f32[4,512]{1,0:T(4,128)S(1)}, f32[4,512]{1,0:T(4,128)S(1)}, u32[]{:S(2)}, u32[]{:S(2)}) %collective-permute-start.7) | collective-permute-done | bytes 8224 | tf_op jit(solution)/shard_map/ppermute | solution.py:35
  204.3 2.8 collective-permute-done.4
  207.2 2.9 convolution_select_fusion.9
  210.0 9.3 %collective-permute-start.5 = (f32[512,512]{1,0:T(8,128)}, f32[512,512]{1,0:T(8,128)}, u32[]{:S(2)}, u32[]{:S(2)}) collective-permute-start(f32[512,512]{1,0:T(8,128)} %convolution_select_fusion.9), channel_id=1, source_target_pairs={{0,32},{1,33},{2,34},{3,35},{4,36},{5,37},{6,38},{7,39},{8,40},{9,... | collective-permute-start | bytes 3145736 | tf_op jit(solution)/shard_map/ppermute | solution.py:35
  222.3 11.1 %collective-permute-done.9 = f32[4,512]{1,0:T(4,128)S(1)} collective-permute-done((f32[4,512]{1,0:T(4,128)S(1)}, f32[4,512]{1,0:T(4,128)S(1)}, u32[]{:S(2)}, u32[]{:S(2)}) %collective-permute-start.9) | collective-permute-done | bytes 8224 | tf_op jit(solution)/shard_map/ppermute | solution.py:35
  233.4 2.2 fusion.43
  235.6 2.1 collective-permute-start.10
  237.7 4.7 convolution_select_fusion.4
  242.4 3.9 collective-permute-start.24
  246.3 14.5 %collective-permute-done.10 = f32[4,512]{1,0:T(4,128)S(1)} collective-permute-done((f32[4,512]{1,0:T(4,128)S(1)}, f32[4,512]{1,0:T(4,128)S(1)}, u32[]{:S(2)}, u32[]{:S(2)}) %collective-permute-start.10) | collective-permute-done | bytes 8224 | tf_op jit(solution)/shard_map/ppermute | solution.py:35
  260.8 2.2 fusion.42
  263.0 18.0 %collective-permute-start.11 = (f32[4,512]{1,0:T(4,128)S(1)}, f32[4,512]{1,0:T(4,128)S(1)}, u32[]{:S(2)}, u32[]{:S(2)}) collective-permute-start(f32[4,512]{1,0:T(4,128)S(1)} %fusion.42), channel_id=1, source_target_pairs={{0,16},{1,17},{2,18},{3,19},{4,20},{5,21},{6,22},{7,23},{8,24},{9,... | collective-permute-start | bytes 24584 | tf_op jit(solution)/shard_map/ppermute | solution.py:35
  281.0 4.7 convolution_select_fusion.8
  288.6 2.5 collective-permute-start.12
  291.1 6.9 %collective-permute-done.12 = f32[4,512]{1,0:T(4,128)S(1)} collective-permute-done((f32[4,512]{1,0:T(4,128)S(1)}, f32[4,512]{1,0:T(4,128)S(1)}, u32[]{:S(2)}, u32[]{:S(2)}) %collective-permute-start.12) | collective-permute-done | bytes 8224 | tf_op jit(solution)/shard_map/ppermute | solution.py:35
  298.0 2.2 fusion.40
  302.1 4.7 convolution_select_fusion.3
  306.8 4.8 collective-permute-start.26
  311.7 2.2 fusion.39
  313.9 3.7 convolution_select_fusion.7
  322.2 2.2 fusion.38
  324.4 4.4 collective-permute-start.15
  328.8 30.4 %collective-permute-done.26 = f32[512,512]{1,0:T(8,128)} collective-permute-done((f32[512,512]{1,0:T(8,128)}, f32[512,512]{1,0:T(8,128)}, u32[]{:S(2)}, u32[]{:S(2)}) %collective-permute-start.26) | collective-permute-done | bytes 1048608 | tf_op jit(solution)/shard_map/ppermute | solution.py:35
  359.3 4.7 convolution_select_fusion.2
  378.5 20.1 %collective-permute-done.16 = f32[4,512]{1,0:T(4,128)S(1)} collective-permute-done((f32[4,512]{1,0:T(4,128)S(1)}, f32[4,512]{1,0:T(4,128)S(1)}, u32[]{:S(2)}, u32[]{:S(2)}) %collective-permute-start.16) | collective-permute-done | bytes 8224 | tf_op jit(solution)/shard_map/ppermute | solution.py:35
  399.6 32.2 %collective-permute-start.17 = (f32[4,512]{1,0:T(4,128)S(1)}, f32[4,512]{1,0:T(4,128)S(1)}, u32[]{:S(2)}, u32[]{:S(2)}) collective-permute-start(f32[4,512]{1,0:T(4,128)S(1)} %fusion.24), channel_id=1, source_target_pairs={{2,0},{3,1},{4,2},{5,3},{6,4},{7,5},{8,6},{9,7},{10,8},{11,9},{12,... | collective-permute-start | bytes 24584 | tf_op jit(solution)/shard_map/ppermute | solution.py:35
  434.1 3.3 collective-permute-start.19
  437.5 3.7 convolution_select_fusion.1
  441.2 2.2 collective-permute-start.30
  443.4 2.2 fusion.22
  445.6 4.6 collective-permute-start.21
  450.2 3.1 collective-permute-done.21
  453.3 2.2 fusion.21
  457.4 6.7 %collective-permute-done.23 = f32[4,512]{1,0:T(4,128)S(1)} collective-permute-done((f32[4,512]{1,0:T(4,128)S(1)}, f32[4,512]{1,0:T(4,128)S(1)}, u32[]{:S(2)}, u32[]{:S(2)}) %collective-permute-start.23) | collective-permute-done | bytes 8224 | tf_op jit(solution)/shard_map/ppermute | solution.py:35
  464.2 2.2 fusion.20
  468.3 8.4 %collective-permute-done.25 = f32[4,512]{1,0:T(4,128)S(1)} collective-permute-done((f32[4,512]{1,0:T(4,128)S(1)}, f32[4,512]{1,0:T(4,128)S(1)}, u32[]{:S(2)}, u32[]{:S(2)}) %collective-permute-start.25) | collective-permute-done | bytes 8224 | tf_op jit(solution)/shard_map/ppermute | solution.py:35
  476.7 2.2 fusion.19
  480.8 3.6 collective-permute-done.27
  488.6 3.9 collective-permute-done.29
  495.3 3.6 collective-permute-done.31
  504.1 9.9 %all_to_all.15 = f32[2,4,4,512]{3,1,0,2:T(4,128)S(1)} all-to-all(f32[2,4,4,512]{3,1,0,2:T(4,128)S(1)} %copy.10), channel_id=1, replica_groups=mesh['tm'=64,'state'=4] {'state'}, dimensions={2} | all-to-all | bytes 131072 | tf_op jit(solution)/shard_map/all_to_all | solution.py:125
  (111 shorter events, 68.0 us)
Async XLA Ops:
  7.2 111.0 %copy-start = (f32[16,4]{0,1:T(4,128)S(1)}, f32[16,4]{0,1:T(4,128)}, u32[]{:S(2)}) copy-start(f32[16,4]{0,1:T(4,128)} %param.9) | copy-start | bytes 772
  7.2 29.6 %all-gather.2.cloned.1.call-start = ((), (), s32[]{:S(2)}) async-start(), calls=%async_computation.1 | async-start | bytes 1310720 | tf_op jit(solution)/shard_map/all_gather | solution.py:51
  7.9 0.8 copy-start.13
  7.9 0.7 copy-start.12
  8.6 0.7 copy-start.11
  36.8 1.2 copy-start.9
  43.9 26.1 %copy-start.7 = (f32[512,512]{1,0:T(8,128)}, f32[512,512]{1,0:T(8,128)S(1)}, u32[]{:S(2)}) copy-start(f32[512,512]{1,0:T(8,128)S(1)} %convolution_multiply_fusion.3) | copy-start | bytes 3145732
  43.9 23.0 %collective-permute-start = (f32[512,512]{1,0:T(8,128)S(1)}, f32[512,512]{1,0:T(8,128)}, u32[]{:S(2)}, u32[]{:S(2)}) collective-permute-start(f32[512,512]{1,0:T(8,128)S(1)} %convolution_multiply_fusion.3), channel_id=1, source_target_pairs={{0,1},{1,2},{2,3},{3,4},{4,5},{5,6},{6,7},{7,8},{8,9},{9,10},{10,1... | collective-permute-start | bytes 3145736 | tf_op jit(solution)/shard_map/ppermute | solution.py:35
  70.1 32.2 %copy-start.1 = (f32[512,512]{1,0:T(8,128)}, f32[512,512]{1,0:T(8,128)S(1)}, u32[]{:S(2)}) copy-start(f32[512,512]{1,0:T(8,128)S(1)} %convolution_select_fusion.13) | copy-start | bytes 3145732
  70.1 29.1 %collective-permute-start.1 = (f32[512,512]{1,0:T(8,128)S(1)}, f32[512,512]{1,0:T(8,128)}, u32[]{:S(2)}, u32[]{:S(2)}) collective-permute-start(f32[512,512]{1,0:T(8,128)S(1)} %convolution_select_fusion.13), channel_id=1, source_target_pairs={{0,2},{1,3},{2,4},{3,5},{4,6},{5,7},{6,8},{7,9},{8,10},{9,11},{10,... | collective-permute-start | bytes 3145736 | tf_op jit(solution)/shard_map/ppermute | solution.py:35
  102.3 16.6 %copy-start.3 = (f32[512,512]{1,0:T(8,128)}, f32[512,512]{1,0:T(8,128)S(1)}, u32[]{:S(2)}) copy-start(f32[512,512]{1,0:T(8,128)S(1)} %convolution_select_fusion.12) | copy-start | bytes 3145732
  102.3 16.6 %collective-permute-start.2 = (f32[512,512]{1,0:T(8,128)S(1)}, f32[512,512]{1,0:T(8,128)S(1)}, u32[]{:S(2)}, u32[]{:S(2)}) collective-permute-start(f32[512,512]{1,0:T(8,128)S(1)} %convolution_select_fusion.12), channel_id=1, source_target_pairs={{0,4},{1,5},{2,6},{3,7},{4,8},{5,9},{6,10},{7,11},{8,12},{9,13},{1... | collective-permute-start | bytes 3145736 | tf_op jit(solution)/shard_map/ppermute | solution.py:35
  115.0 27.5 %collective-permute-start.18 = (f32[512,512]{1,0:T(8,128)S(1)}, f32[512,512]{1,0:T(8,128)}, u32[]{:S(2)}, u32[]{:S(2)}) collective-permute-start(f32[512,512]{1,0:T(8,128)S(1)} %fusion.5), channel_id=1, source_target_pairs={{1,0},{2,1},{3,2},{4,3},{5,4},{6,5},{7,6},{8,7},{9,8},{10,9},{11,1... | collective-permute-start | bytes 3145736 | tf_op jit(solution)/shard_map/ppermute | solution.py:35
  121.8 31.3 %collective-permute-start.3 = (f32[512,512]{1,0:T(8,128)}, f32[512,512]{1,0:T(8,128)}, u32[]{:S(2)}, u32[]{:S(2)}) collective-permute-start(f32[512,512]{1,0:T(8,128)} %convolution_select_fusion.11), channel_id=1, source_target_pairs={{0,8},{1,9},{2,10},{3,11},{4,12},{5,13},{6,14},{7,15},{8,16},{9,17... | collective-permute-start | bytes 3145736 | tf_op jit(solution)/shard_map/ppermute | solution.py:35
  145.5 29.5 %collective-permute-start.20 = (f32[512,512]{1,0:T(8,128)S(1)}, f32[512,512]{1,0:T(8,128)S(1)}, u32[]{:S(2)}, u32[]{:S(2)}) collective-permute-start(f32[512,512]{1,0:T(8,128)S(1)} %convolution_select_fusion.6), channel_id=1, source_target_pairs={{2,0},{3,1},{4,2},{5,3},{6,4},{7,5},{8,6},{9,7},{10,8},{11,9},{12,... | collective-permute-start | bytes 3145736 | tf_op jit(solution)/shard_map/ppermute | solution.py:35
  156.8 50.4 %copy-start.4 = (f32[512,512]{1,0:T(8,128)}, f32[512,512]{1,0:T(8,128)S(1)}, u32[]{:S(2)}) copy-start(f32[512,512]{1,0:T(8,128)S(1)} %convolution_select_fusion.10) | copy-start | bytes 3145732
  156.8 50.4 %collective-permute-start.4 = (f32[512,512]{1,0:T(8,128)S(1)}, f32[512,512]{1,0:T(8,128)S(1)}, u32[]{:S(2)}, u32[]{:S(2)}) collective-permute-start(f32[512,512]{1,0:T(8,128)S(1)} %convolution_select_fusion.10), channel_id=1, source_target_pairs={{0,16},{1,17},{2,18},{3,19},{4,20},{5,21},{6,22},{7,23},{8,24},{9,... | collective-permute-start | bytes 3145736 | tf_op jit(solution)/shard_map/ppermute | solution.py:35
  162.0 39.3 %copy-start.8 = (f32[512,512]{1,0:T(8,128)S(1)}, f32[512,512]{1,0:T(8,128)}, u32[]{:S(2)}) copy-start(f32[512,512]{1,0:T(8,128)} %copy-done.7) | copy-start | bytes 3145732
  162.0 39.3 %collective-permute-start.7 = (f32[4,512]{1,0:T(4,128)S(1)}, f32[4,512]{1,0:T(4,128)S(1)}, u32[]{:S(2)}, u32[]{:S(2)}) collective-permute-start(f32[4,512]{1,0:T(4,128)S(1)} %fusion.46), channel_id=1, source_target_pairs={{0,1},{1,2},{2,3},{3,4},{4,5},{5,6},{6,7},{7,8},{8,9},{9,10},{10,1... | collective-permute-start | bytes 24584 | tf_op jit(solution)/shard_map/ppermute | solution.py:35
  177.9 59.8 %collective-permute-start.22 = (f32[512,512]{1,0:T(8,128)}, f32[512,512]{1,0:T(8,128)}, u32[]{:S(2)}, u32[]{:S(2)}) collective-permute-start(f32[512,512]{1,0:T(8,128)} %convolution_select_fusion.5), channel_id=1, source_target_pairs={{4,0},{5,1},{6,2},{7,3},{8,4},{9,5},{10,6},{11,7},{12,8},{13,9},{1... | collective-permute-start | bytes 3145736 | tf_op jit(solution)/shard_map/ppermute | solution.py:35
  202.3 17.1 %copy-start.2 = (f32[512,512]{1,0:T(8,128)S(1)}, f32[512,512]{1,0:T(8,128)}, u32[]{:S(2)}) copy-start(f32[512,512]{1,0:T(8,128)} %copy-done.1) | copy-start | bytes 3145732
  202.3 17.1 %collective-permute-start.8 = (f32[4,512]{1,0:T(4,128)S(1)}, f32[4,512]{1,0:T(4,128)S(1)}, u32[]{:S(2)}, u32[]{:S(2)}) collective-permute-start(f32[4,512]{1,0:T(4,128)S(1)} %fusion.45), channel_id=1, source_target_pairs={{0,2},{1,3},{2,4},{3,5},{4,6},{5,7},{6,8},{7,9},{8,10},{9,11},{10,... | collective-permute-start | bytes 24584 | tf_op jit(solution)/shard_map/ppermute | solution.py:35
  210.0 70.9 %collective-permute-start.5 = (f32[512,512]{1,0:T(8,128)}, f32[512,512]{1,0:T(8,128)}, u32[]{:S(2)}, u32[]{:S(2)}) collective-permute-start(f32[512,512]{1,0:T(8,128)} %convolution_select_fusion.9), channel_id=1, source_target_pairs={{0,32},{1,33},{2,34},{3,35},{4,36},{5,37},{6,38},{7,39},{8,40},{9,... | collective-permute-start | bytes 3145736 | tf_op jit(solution)/shard_map/ppermute | solution.py:35
  220.4 13.0 %collective-permute-start.9 = (f32[4,512]{1,0:T(4,128)S(1)}, f32[4,512]{1,0:T(4,128)S(1)}, u32[]{:S(2)}, u32[]{:S(2)}) collective-permute-start(f32[4,512]{1,0:T(4,128)S(1)} %fusion.44), channel_id=1, source_target_pairs={{0,4},{1,5},{2,6},{3,7},{4,8},{5,9},{6,10},{7,11},{8,12},{9,13},{1... | collective-permute-start | bytes 24584 | tf_op jit(solution)/shard_map/ppermute | solution.py:35
  235.6 25.2 %collective-permute-start.10 = (f32[4,512]{1,0:T(4,128)S(1)}, f32[4,512]{1,0:T(4,128)S(1)}, u32[]{:S(2)}, u32[]{:S(2)}) collective-permute-start(f32[4,512]{1,0:T(4,128)S(1)} %fusion.43), channel_id=1, source_target_pairs={{0,8},{1,9},{2,10},{3,11},{4,12},{5,13},{6,14},{7,15},{8,16},{9,17... | collective-permute-start | bytes 24584 | tf_op jit(solution)/shard_map/ppermute | solution.py:35
  242.4 59.8 %collective-permute-start.24 = (f32[512,512]{1,0:T(8,128)}, f32[512,512]{1,0:T(8,128)}, u32[]{:S(2)}, u32[]{:S(2)}) collective-permute-start(f32[512,512]{1,0:T(8,128)} %convolution_select_fusion.4), channel_id=1, source_target_pairs={{8,0},{9,1},{10,2},{11,3},{12,4},{13,5},{14,6},{15,7},{16,8},{17,9... | collective-permute-start | bytes 3145736 | tf_op jit(solution)/shard_map/ppermute | solution.py:35
  262.9 24.6 %copy-start.5 = (f32[512,512]{1,0:T(8,128)S(1)}, f32[512,512]{1,0:T(8,128)}, u32[]{:S(2)}) copy-start(f32[512,512]{1,0:T(8,128)} %copy-done.4) | copy-start | bytes 3145732
  263.0 24.6 %collective-permute-start.11 = (f32[4,512]{1,0:T(4,128)S(1)}, f32[4,512]{1,0:T(4,128)S(1)}, u32[]{:S(2)}, u32[]{:S(2)}) collective-permute-start(f32[4,512]{1,0:T(4,128)S(1)} %fusion.42), channel_id=1, source_target_pairs={{0,16},{1,17},{2,18},{3,19},{4,20},{5,21},{6,22},{7,23},{8,24},{9,... | collective-permute-start | bytes 24584 | tf_op jit(solution)/shard_map/ppermute | solution.py:35
  285.7 28.2 %collective-permute-start.6 = (f32[512,512]{1,0:T(8,128)}, f32[512,512]{1,0:T(8,128)}, u32[]{:S(2)}, u32[]{:S(2)}) collective-permute-start(f32[512,512]{1,0:T(8,128)} %convolution_select_fusion.8), channel_id=1, source_target_pairs={{0,64},{1,65},{2,66},{3,67},{4,68},{5,69},{6,70},{7,71},{8,72},{9,... | collective-permute-start | bytes 3145736 | tf_op jit(solution)/shard_map/ppermute | solution.py:35
  288.6 9.5 %collective-permute-start.12 = (f32[4,512]{1,0:T(4,128)S(1)}, f32[4,512]{1,0:T(4,128)S(1)}, u32[]{:S(2)}, u32[]{:S(2)}) collective-permute-start(f32[4,512]{1,0:T(4,128)S(1)} %fusion.41), channel_id=1, source_target_pairs={{0,32},{1,33},{2,34},{3,35},{4,36},{5,37},{6,38},{7,39},{8,40},{9,... | collective-permute-start | bytes 24584 | tf_op jit(solution)/shard_map/ppermute | solution.py:35
  300.2 11.5 %collective-permute-start.13 = (f32[4,512]{1,0:T(4,128)S(1)}, f32[4,512]{1,0:T(4,128)S(1)}, u32[]{:S(2)}, u32[]{:S(2)}) collective-permute-start(f32[4,512]{1,0:T(4,128)S(1)} %fusion.40), channel_id=1, source_target_pairs={{0,64},{1,65},{2,66},{3,67},{4,68},{5,69},{6,70},{7,71},{8,72},{9,... | collective-permute-start | bytes 24584 | tf_op jit(solution)/shard_map/ppermute | solution.py:35
  306.8 52.4 %collective-permute-start.26 = (f32[512,512]{1,0:T(8,128)}, f32[512,512]{1,0:T(8,128)}, u32[]{:S(2)}, u32[]{:S(2)}) collective-permute-start(f32[512,512]{1,0:T(8,128)} %convolution_select_fusion.3), channel_id=1, source_target_pairs={{16,0},{17,1},{18,2},{19,3},{20,4},{21,5},{22,6},{23,7},{24,8},{25... | collective-permute-start | bytes 3145736 | tf_op jit(solution)/shard_map/ppermute | solution.py:35
  313.9 4.7 copy-start.10
  317.6 1.0 copy-start.6
  319.6 2.7 collective-permute-start.14
  324.4 41.5 %collective-permute-start.15 = (f32[4,512]{1,0:T(4,128)S(1)}, f32[4,512]{1,0:T(4,128)S(1)}, u32[]{:S(2)}, u32[]{:S(2)}) collective-permute-start(f32[4,512]{1,0:T(4,128)S(1)} %fusion.38), channel_id=1, source_target_pairs={{0,1},{1,2},{2,3},{3,4},{4,5},{5,6},{6,7},{7,8},{8,9},{9,10},{10,1... | collective-permute-start | bytes 24584 | tf_op jit(solution)/shard_map/ppermute | solution.py:35
  364.0 73.5 %collective-permute-start.28 = (f32[512,512]{1,0:T(8,128)}, f32[512,512]{1,0:T(8,128)}, u32[]{:S(2)}, u32[]{:S(2)}) collective-permute-start(f32[512,512]{1,0:T(8,128)} %convolution_select_fusion.2), channel_id=1, source_target_pairs={{32,0},{33,1},{34,2},{35,3},{36,4},{37,5},{38,6},{39,7},{40,8},{41... | collective-permute-start | bytes 3145736 | tf_op jit(solution)/shard_map/ppermute | solution.py:35
  376.6 22.0 %collective-permute-start.16 = (f32[4,512]{1,0:T(4,128)S(1)}, f32[4,512]{1,0:T(4,128)S(1)}, u32[]{:S(2)}, u32[]{:S(2)}) collective-permute-start(f32[4,512]{1,0:T(4,128)S(1)} %fusion.26), channel_id=1, source_target_pairs={{1,0},{2,1},{3,2},{4,3},{5,4},{6,5},{7,6},{8,7},{9,8},{10,9},{11,1... | collective-permute-start | bytes 24584 | tf_op jit(solution)/shard_map/ppermute | solution.py:35
  399.6 33.6 %collective-permute-start.17 = (f32[4,512]{1,0:T(4,128)S(1)}, f32[4,512]{1,0:T(4,128)S(1)}, u32[]{:S(2)}, u32[]{:S(2)}) collective-permute-start(f32[4,512]{1,0:T(4,128)S(1)} %fusion.24), channel_id=1, source_target_pairs={{2,0},{3,1},{4,2},{5,3},{6,4},{7,5},{8,6},{9,7},{10,8},{11,9},{12,... | collective-permute-start | bytes 24584 | tf_op jit(solution)/shard_map/ppermute | solution.py:35
  434.1 9.2 %collective-permute-start.19 = (f32[4,512]{1,0:T(4,128)S(1)}, f32[4,512]{1,0:T(4,128)S(1)}, u32[]{:S(2)}, u32[]{:S(2)}) collective-permute-start(f32[4,512]{1,0:T(4,128)S(1)} %fusion.23), channel_id=1, source_target_pairs={{4,0},{5,1},{6,2},{7,3},{8,4},{9,5},{10,6},{11,7},{12,8},{13,9},{1... | collective-permute-start | bytes 24584 | tf_op jit(solution)/shard_map/ppermute | solution.py:35
  441.2 45.5 %collective-permute-start.30 = (f32[512,512]{1,0:T(8,128)S(1)}, f32[512,512]{1,0:T(8,128)S(1)}, u32[]{:S(2)}, u32[]{:S(2)}) collective-permute-start(f32[512,512]{1,0:T(8,128)S(1)} %convolution_select_fusion.1), channel_id=1, source_target_pairs={{64,0},{65,1},{66,2},{67,3},{68,4},{69,5},{70,6},{71,7},{72,8},{73... | collective-permute-start | bytes 3145736 | tf_op jit(solution)/shard_map/ppermute | solution.py:35
  445.6 7.8 %collective-permute-start.21 = (f32[4,512]{1,0:T(4,128)S(1)}, f32[4,512]{1,0:T(4,128)S(1)}, u32[]{:S(2)}, u32[]{:S(2)}) collective-permute-start(f32[4,512]{1,0:T(4,128)S(1)} %fusion.22), channel_id=1, source_target_pairs={{8,0},{9,1},{10,2},{11,3},{12,4},{13,5},{14,6},{15,7},{16,8},{17,9... | collective-permute-start | bytes 24584 | tf_op jit(solution)/shard_map/ppermute | solution.py:35
  455.5 8.7 %collective-permute-start.23 = (f32[4,512]{1,0:T(4,128)S(1)}, f32[4,512]{1,0:T(4,128)S(1)}, u32[]{:S(2)}, u32[]{:S(2)}) collective-permute-start(f32[4,512]{1,0:T(4,128)S(1)} %fusion.21), channel_id=1, source_target_pairs={{16,0},{17,1},{18,2},{19,3},{20,4},{21,5},{22,6},{23,7},{24,8},{25... | collective-permute-start | bytes 24584 | tf_op jit(solution)/shard_map/ppermute | solution.py:35
  466.4 10.4 %collective-permute-start.25 = (f32[4,512]{1,0:T(4,128)S(1)}, f32[4,512]{1,0:T(4,128)S(1)}, u32[]{:S(2)}, u32[]{:S(2)}) collective-permute-start(f32[4,512]{1,0:T(4,128)S(1)} %fusion.20), channel_id=1, source_target_pairs={{32,0},{33,1},{34,2},{35,3},{36,4},{37,5},{38,6},{39,7},{40,8},{41... | collective-permute-start | bytes 24584 | tf_op jit(solution)/shard_map/ppermute | solution.py:35
  478.9 5.5 %collective-permute-start.27 = (f32[4,512]{1,0:T(4,128)S(1)}, f32[4,512]{1,0:T(4,128)S(1)}, u32[]{:S(2)}, u32[]{:S(2)}) collective-permute-start(f32[4,512]{1,0:T(4,128)S(1)} %fusion.19), channel_id=1, source_target_pairs={{64,0},{65,1},{66,2},{67,3},{68,4},{69,5},{70,6},{71,7},{72,8},{73... | collective-permute-start | bytes 24584 | tf_op jit(solution)/shard_map/ppermute | solution.py:35
  485.4 7.1 %collective-permute-start.29 = (f32[4,512]{1,0:T(4,128)S(1)}, f32[4,512]{1,0:T(4,128)S(1)}, u32[]{:S(2)}, u32[]{:S(2)}) collective-permute-start(f32[4,512]{1,0:T(4,128)S(1)} %fusion.18), channel_id=1, source_target_pairs={{128,0},{129,1},{130,2},{131,3},{132,4},{133,5},{134,6},{135,7},{1... | collective-permute-start | bytes 24584 | tf_op jit(solution)/shard_map/ppermute | solution.py:35
  493.4 5.5 %collective-permute-start.31 = (f32[4,512]{1,0:T(4,128)S(1)}, f32[4,512]{1,0:T(4,128)S(1)}, u32[]{:S(2)}, u32[]{:S(2)}) collective-permute-start(f32[4,512]{1,0:T(4,128)S(1)} %fusion.17), channel_id=1, source_target_pairs={{1,0},{2,1},{3,2},{4,3},{5,4},{6,5},{7,6},{8,7},{9,8},{10,9},{11,1... | collective-permute-start | bytes 24584 | tf_op jit(solution)/shard_map/ppermute | solution.py:35
Sparse Core Ops, SparseCore 0:
  9.8 26.9 all-gather.1
where the time goes:
time: 532 us; the launch traced here: 523 us
  waiting for transfers between devices  234 us (44%)
  starting transfers between devices  143 us (27%)
  matrix products  111 us (21%)
  between operations  15.2 us (3%)
  blocking collectives  9.88 us (2%)
  local copies, waits for them, and re-layouts  6.3 us (1%)
    ppermute x32, waiting for transfers between devices, shifted(): return lax.ppermute(block, AXES, route)  206 us
    ppermute x32, starting transfers between devices, shifted(): return lax.ppermute(block, AXES, route)  143 us
    dot_general x26, matrix products, product(): jnp.dot(left, right, precision=lax.Precision.HIGHEST, preferred_element_t...  66.1 us
    dot_general x25, matrix products, transposed(): lax.dot_general(left, right, (((1,), (1,)), ((), ())), precision=lax.Prec...  35.1 us
    all_gather x1, waiting for transfers between devices, per_device(): lax.all_gather(dynamics, 'state', axis=0, tiled=True) * block_mask  27.4 us
  transfers between devices with their start and end apart: 33, of which 20 were waited for; matrix products, arithmetic and copies ran while one was open for 19% of the time, Pallas kernels for 0%

commit v1 on v0

--- a/solution.py
+++ b/solution.py
@@ -36,6 +36,26 @@
 
 
 def per_device(dynamics, pattern, initial_mean, observed, obs_index, obs_noise):
+
+    def _finish_stages_all(field_in):
+        dev_count = lax.axis_size("state")
+        entries = []
+        for rr in [*range(dev_count)]:
+            entries.append((rr, (rr + 1) % dev_count))
+        sheets = []
+        for rr in tuple(range(dev_count)):
+            sheets.append((rr, (rr - 1) % dev_count))
+        passed, later = ([field_in], [field_in])
+        for _ in range(dev_count // 2):
+            passed.append(lax.ppermute(passed[-1], axis_name="state", perm=entries))
+        for _ in [*range((dev_count - 1) // 2)]:
+            later.append(lax.ppermute(later[-1], perm=sheets, axis_name="state"))
+        piece_now = jnp.concatenate([*passed[::-1], *later[1:]], axis=0)
+        seen_now = jnp.roll(
+            piece_now, (lax.axis_index("state") - dev_count // 2) * field_in.shape[0], 0
+        )
+        return seen_now
+
     state_width = dynamics.shape[1]
     blocks = pattern.shape[0]
     block_span = state_width // blocks
@@ -48,7 +68,7 @@
     steps_total = span * segments
     present = jnp.maximum(pattern, jnp.eye(blocks, dtype=jnp.int32))
     block_mask = jnp.repeat(jnp.repeat(present, block_span, 0), block_span, 1).astype(jnp.float32)
-    transition = lax.all_gather(dynamics, "state", axis=0, tiled=True) * block_mask
+    transition = _finish_stages_all(dynamics) * block_mask
     first = member * span
     obs_here = lax.dynamic_slice_in_dim(observed, first, span, 0)
     index_here = lax.dynamic_slice_in_dim(obs_index, first, span, 0)

time: 532 us -> 501 us (0.942)
  waiting for transfers between devices: 234 us -> 217 us
  between operations: 15.2 us -> 1.88 us
  starting transfers between devices: 143 us -> 135 us
  blocking collectives: 9.88 us -> 16.9 us
    all_gather x1 -> x0, waiting for transfers between devices: 27.4 us -> none  [per_device(): lax.all_gather(dynamics, 'state', axis=0, tiled=True) * block_mask]
    ppermute x0 -> x3, waiting for transfers between devices: none -> 12.1 us  [the longest x2 12.1 us: _finish_stages_all(): passed.append(lax.ppermute(passed[-1], axis_name='state', perm=entries))]
    ppermute x32, starting transfers between devices: 143 us -> 131 us  [shifted(): return lax.ppermute(block, AXES, route)]
    all_to_all x1, blocking collectives: 9.88 us -> 16.9 us  [per_device(): lax.all_to_all(both, 'state', split_axis=2, concat_axis=1, tiled=True)]
  transfers between devices with their start and end apart: 33 -> 35, of which waited for: 20 -> 20; matrix products, arithmetic and copies ran while one was open for 19% -> 20% of each run, Pallas kernels for 0% -> 0%
where the time goes in v1:
time: 501 us; the launch traced here: 492 us
  waiting for transfers between devices  217 us (43%)
  starting transfers between devices  135 us (27%)
  matrix products  111 us (22%)
  blocking collectives  16.9 us (3%)
  local copies, waits for them, and re-layouts  6.29 us (1%)
    ppermute x32, waiting for transfers between devices, shifted(): return lax.ppermute(block, AXES, route)  204 us
    ppermute x32, starting transfers between devices, shifted(): return lax.ppermute(block, AXES, route)  131 us
    dot_general x26, matrix products, product(): jnp.dot(left, right, precision=lax.Precision.HIGHEST, preferred_element_t...  65.9 us
    dot_general x25, matrix products, transposed(): lax.dot_general(left, right, (((1,), (1,)), ((), ())), precision=lax.Prec...  35.1 us
    all_to_all x1, blocking collectives, per_device(): lax.all_to_all(both, 'state', split_axis=2, concat_axis=1, tiled=True)  16.9 us
    ppermute x2, waiting for transfers between devices, _finish_stages_all(): passed.append(lax.ppermute(passed[-1], axis_name='state', perm=entries))  12.1 us
  transfers between devices with their start and end apart: 35, of which 20 were waited for; matrix products, arithmetic and copies ran while one was open for 20% of the time, Pallas kernels for 0%

profile of v1, /device:TPU:232, one launch (start us, length us, event | category | flops | bytes accessed | tf_op | source)
XLA Modules:
  0.0 492.1 jit_solution(306803109408773723)
XLA Ops:
  5.5 4.7 collective-permute-done
  11.2 7.4 %collective-permute-done.1 = f32[128,512]{1,0:T(8,128)S(1)} collective-permute-done((f32[128,512]{1,0:T(8,128)S(1)}, f32[128,512]{1,0:T(8,128)S(1)}, u32[]{:S(2)}, u32[]{:S(2)}) %collective-permute-start.1) | collective-permute-done | bytes 262176 | tf_op jit(solution)/shard_map/ppermute | solution.py:50
  20.6 2.0 fusion.2
  28.3 21.0 %collective-permute-done.3 = f32[512,512]{1,0:T(8,128)} collective-permute-done((f32[512,512]{1,0:T(8,128)S(1)}, f32[512,512]{1,0:T(8,128)}, u32[]{:S(2)}, u32[]{:S(2)}) %collective-permute-start.3) | collective-permute-done | bytes 1048608 | tf_op jit(solution)/shard_map/ppermute | solution.py:35
  49.2 3.1 convolution_select_fusion.13
  52.3 5.0 %collective-permute-start.4 = (f32[512,512]{1,0:T(8,128)S(1)}, f32[512,512]{1,0:T(8,128)}, u32[]{:S(2)}, u32[]{:S(2)}) collective-permute-start(f32[512,512]{1,0:T(8,128)S(1)} %convolution_select_fusion.13), channel_id=1, source_target_pairs={{0,2},{1,3},{2,4},{3,5},{4,6},{5,7},{6,8},{7,9},{8,10},{9,11},{10,... | collective-permute-start | bytes 3145736 | tf_op jit(solution)/shard_map/ppermute | solution.py:35
  58.0 22.3 %collective-permute-done.4 = f32[512,512]{1,0:T(8,128)} collective-permute-done((f32[512,512]{1,0:T(8,128)S(1)}, f32[512,512]{1,0:T(8,128)}, u32[]{:S(2)}, u32[]{:S(2)}) %collective-permute-start.4) | collective-permute-done | bytes 1048608 | tf_op jit(solution)/shard_map/ppermute | solution.py:35
  80.3 3.1 convolution_select_fusion.12
  83.4 3.6 collective-permute-start.5
  87.0 4.8 fusion.7
  91.8 2.6 fusion.6
  94.4 2.5 fusion.5
  96.9 2.4 collective-permute-start.21
  100.1 2.9 convolution_select_fusion.11
  103.0 5.4 %collective-permute-start.6 = (f32[512,512]{1,0:T(8,128)}, f32[512,512]{1,0:T(8,128)}, u32[]{:S(2)}, u32[]{:S(2)}) collective-permute-start(f32[512,512]{1,0:T(8,128)} %convolution_select_fusion.11), channel_id=1, source_target_pairs={{0,8},{1,9},{2,10},{3,11},{4,12},{5,13},{6,14},{7,15},{8,16},{9,17... | collective-permute-start | bytes 3145736 | tf_op jit(solution)/shard_map/ppermute | solution.py:35
  108.5 2.8 multiply_reduce_fusion
  111.3 12.7 %collective-permute-done.21 = f32[512,512]{1,0:T(8,128)} collective-permute-done((f32[512,512]{1,0:T(8,128)S(1)}, f32[512,512]{1,0:T(8,128)}, u32[]{:S(2)}, u32[]{:S(2)}) %collective-permute-start.21) | collective-permute-done | bytes 1048608 | tf_op jit(solution)/shard_map/ppermute | solution.py:35
  124.0 3.1 convolution_select_fusion.6
  127.1 5.6 %collective-permute-start.23 = (f32[512,512]{1,0:T(8,128)S(1)}, f32[512,512]{1,0:T(8,128)S(1)}, u32[]{:S(2)}, u32[]{:S(2)}) collective-permute-start(f32[512,512]{1,0:T(8,128)S(1)} %convolution_select_fusion.6), channel_id=1, source_target_pairs={{2,0},{3,1},{4,2},{5,3},{6,4},{7,5},{8,6},{9,7},{10,8},{11,9},{12,... | collective-permute-start | bytes 3145736 | tf_op jit(solution)/shard_map/ppermute | solution.py:35
  133.7 3.8 convolution_select_fusion.10
  141.3 1.9 collective-permute-start.10
  143.3 11.6 %collective-permute-done.23 = f32[512,512]{1,0:T(8,128)S(1)} collective-permute-done((f32[512,512]{1,0:T(8,128)S(1)}, f32[512,512]{1,0:T(8,128)S(1)}, u32[]{:S(2)}, u32[]{:S(2)}) %collective-permute-start.23) | collective-permute-done | bytes 1048608 | tf_op jit(solution)/shard_map/ppermute | solution.py:35
  154.8 2.9 convolution_select_fusion.5
  157.7 3.5 collective-permute-start.25
  161.2 25.2 %collective-permute-done.10 = f32[4,512]{1,0:T(4,128)S(1)} collective-permute-done((f32[4,512]{1,0:T(4,128)S(1)}, f32[4,512]{1,0:T(4,128)S(1)}, u32[]{:S(2)}, u32[]{:S(2)}) %collective-permute-start.10) | collective-permute-done | bytes 8224 | tf_op jit(solution)/shard_map/ppermute | solution.py:35
  189.3 2.9 convolution_select_fusion.9
  192.2 6.7 %collective-permute-start.8 = (f32[512,512]{1,0:T(8,128)}, f32[512,512]{1,0:T(8,128)}, u32[]{:S(2)}, u32[]{:S(2)}) collective-permute-start(f32[512,512]{1,0:T(8,128)} %convolution_select_fusion.9), channel_id=1, source_target_pairs={{0,32},{1,33},{2,34},{3,35},{4,36},{5,37},{6,38},{7,39},{8,40},{9,... | collective-permute-start | bytes 3145736 | tf_op jit(solution)/shard_map/ppermute | solution.py:35
  199.9 2.1 collective-permute-start.12
  202.0 20.4 %collective-permute-done.12 = f32[4,512]{1,0:T(4,128)S(1)} collective-permute-done((f32[4,512]{1,0:T(4,128)S(1)}, f32[4,512]{1,0:T(4,128)S(1)}, u32[]{:S(2)}, u32[]{:S(2)}) %collective-permute-start.12) | collective-permute-done | bytes 8224 | tf_op jit(solution)/shard_map/ppermute | solution.py:35
  222.4 2.2 fusion.43
  226.5 4.7 convolution_select_fusion.4
  231.2 4.0 collective-permute-start.27
  235.3 7.9 %collective-permute-done.13 = f32[4,512]{1,0:T(4,128)S(1)} collective-permute-done((f32[4,512]{1,0:T(4,128)S(1)}, f32[4,512]{1,0:T(4,128)S(1)}, u32[]{:S(2)}, u32[]{:S(2)}) %collective-permute-start.13) | collective-permute-done | bytes 8224 | tf_op jit(solution)/shard_map/ppermute | solution.py:35
  243.2 2.2 fusion.42
  245.4 17.1 %collective-permute-start.14 = (f32[4,512]{1,0:T(4,128)S(1)}, f32[4,512]{1,0:T(4,128)S(1)}, u32[]{:S(2)}, u32[]{:S(2)}) collective-permute-start(f32[4,512]{1,0:T(4,128)S(1)} %fusion.42), channel_id=1, source_target_pairs={{0,16},{1,17},{2,18},{3,19},{4,20},{5,21},{6,22},{7,23},{8,24},{9,... | collective-permute-start | bytes 24584 | tf_op jit(solution)/shard_map/ppermute | solution.py:35
  262.5 4.7 convolution_select_fusion.8
  270.1 4.0 collective-permute-start.15
  274.1 5.4 %collective-permute-done.15 = f32[4,512]{1,0:T(4,128)S(1)} collective-permute-done((f32[4,512]{1,0:T(4,128)S(1)}, f32[4,512]{1,0:T(4,128)S(1)}, u32[]{:S(2)}, u32[]{:S(2)}) %collective-permute-start.15) | collective-permute-done | bytes 8224 | tf_op jit(solution)/shard_map/ppermute | solution.py:35
  279.5 2.2 fusion.40
  283.6 4.7 convolution_select_fusion.3
  288.3 5.1 %collective-permute-start.29 = (f32[512,512]{1,0:T(8,128)}, f32[512,512]{1,0:T(8,128)}, u32[]{:S(2)}, u32[]{:S(2)}) collective-permute-start(f32[512,512]{1,0:T(8,128)} %convolution_select_fusion.3), channel_id=1, source_target_pairs={{16,0},{17,1},{18,2},{19,3},{20,4},{21,5},{22,6},{23,7},{24,8},{25... | collective-permute-start | bytes 3145736 | tf_op jit(solution)/shard_map/ppermute | solution.py:35
  293.4 2.2 fusion.39
  295.6 3.7 convolution_select_fusion.7
  304.0 2.2 fusion.38
  308.1 30.7 %collective-permute-done.29 = f32[512,512]{1,0:T(8,128)} collective-permute-done((f32[512,512]{1,0:T(8,128)}, f32[512,512]{1,0:T(8,128)}, u32[]{:S(2)}, u32[]{:S(2)}) %collective-permute-start.29) | collective-permute-done | bytes 1048608 | tf_op jit(solution)/shard_map/ppermute | solution.py:35
  338.8 4.7 convolution_select_fusion.2
  356.0 2.4 collective-permute-start.19
  358.4 20.2 %collective-permute-done.19 = f32[4,512]{1,0:T(4,128)S(1)} collective-permute-done((f32[4,512]{1,0:T(4,128)S(1)}, f32[4,512]{1,0:T(4,128)S(1)}, u32[]{:S(2)}, u32[]{:S(2)}) %collective-permute-start.19) | collective-permute-done | bytes 8224 | tf_op jit(solution)/shard_map/ppermute | solution.py:35
  379.6 9.6 %collective-permute-start.20 = (f32[4,512]{1,0:T(4,128)S(1)}, f32[4,512]{1,0:T(4,128)S(1)}, u32[]{:S(2)}, u32[]{:S(2)}) collective-permute-start(f32[4,512]{1,0:T(4,128)S(1)} %fusion.24), channel_id=1, source_target_pairs={{2,0},{3,1},{4,2},{5,3},{6,4},{7,5},{8,6},{9,7},{10,8},{11,9},{12,... | collective-permute-start | bytes 24584 | tf_op jit(solution)/shard_map/ppermute | solution.py:35
  391.5 4.3 collective-permute-start.22
  395.8 3.7 convolution_select_fusion.1
  401.5 2.2 fusion.22
  403.7 17.8 %collective-permute-start.24 = (f32[4,512]{1,0:T(4,128)S(1)}, f32[4,512]{1,0:T(4,128)S(1)}, u32[]{:S(2)}, u32[]{:S(2)}) collective-permute-start(f32[4,512]{1,0:T(4,128)S(1)} %fusion.22), channel_id=1, source_target_pairs={{8,0},{9,1},{10,2},{11,3},{12,4},{13,5},{14,6},{15,7},{16,8},{17,9... | collective-permute-start | bytes 24584 | tf_op jit(solution)/shard_map/ppermute | solution.py:35
  422.8 2.2 fusion.21
  425.0 3.6 collective-permute-start.26
  428.6 4.9 collective-permute-done.26
  433.5 2.2 fusion.20
  435.7 3.0 collective-permute-start.28
  438.8 7.3 %collective-permute-done.28 = f32[4,512]{1,0:T(4,128)S(1)} collective-permute-done((f32[4,512]{1,0:T(4,128)S(1)}, f32[4,512]{1,0:T(4,128)S(1)}, u32[]{:S(2)}, u32[]{:S(2)}) %collective-permute-start.28) | collective-permute-done | bytes 8224 | tf_op jit(solution)/shard_map/ppermute | solution.py:35
  446.1 2.2 fusion.19
  450.2 3.6 collective-permute-done.30
  457.9 3.9 collective-permute-done.32
  464.7 3.6 collective-permute-done.34
  473.4 16.9 %all_to_all.15 = f32[2,4,4,512]{3,1,0,2:T(4,128)S(1)} all-to-all(f32[2,4,4,512]{3,1,0,2:T(4,128)S(1)} %copy.10), channel_id=1, replica_groups=mesh['tm'=64,'state'=4] {'state'}, dimensions={2} | all-to-all | bytes 131072 | tf_op jit(solution)/shard_map/all_to_all | solution.py:145
  (116 shorter events, 71.2 us)
Async XLA Ops:
  0.6 98.7 %copy-start = (f32[16,4]{0,1:T(4,128)S(1)}, f32[16,4]{0,1:T(4,128)}, u32[]{:S(2)}) copy-start(f32[16,4]{0,1:T(4,128)} %param.9) | copy-start | bytes 772
  0.6 19.1 %copy-start.9 = (f32[128,512]{1,0:T(8,128)S(1)}, f32[128,512]{1,0:T(8,128)}, u32[]{:S(2)}) copy-start(f32[128,512]{1,0:T(8,128)} %param.6) | copy-start | bytes 786436
  0.7 9.5 %collective-permute-start = (f32[128,512]{1,0:T(8,128)}, f32[128,512]{1,0:T(8,128)S(1)}, u32[]{:S(2)}, u32[]{:S(2)}) collective-permute-start(f32[128,512]{1,0:T(8,128)} %param.6), channel_id=1, source_target_pairs={{0,1},{1,2},{2,3},{3,0},{4,5},{5,6},{6,7},{7,4},{8,9},{9,10},{10,1... | collective-permute-start | bytes 786440 | tf_op jit(solution)/shard_map/ppermute | solution.py:50
  2.2 17.4 %collective-permute-start.2 = (f32[128,512]{1,0:T(8,128)}, f32[128,512]{1,0:T(8,128)S(1)}, u32[]{:S(2)}, u32[]{:S(2)}) collective-permute-start(f32[128,512]{1,0:T(8,128)} %param.6), channel_id=1, source_target_pairs={{0,3},{1,0},{2,1},{3,2},{4,7},{5,4},{6,5},{7,6},{8,11},{9,8},{10,9... | collective-permute-start | bytes 786440 | tf_op jit(solution)/shard_map/ppermute | solution.py:52
  10.2 8.4 %collective-permute-start.1 = (f32[128,512]{1,0:T(8,128)S(1)}, f32[128,512]{1,0:T(8,128)S(1)}, u32[]{:S(2)}, u32[]{:S(2)}) collective-permute-start(f32[128,512]{1,0:T(8,128)S(1)} %collective-permute-done), channel_id=1, source_target_pairs={{0,1},{1,2},{2,3},{3,0},{4,5},{5,6},{6,7},{7,4},{8,9},{9,10},{10,1... | collective-permute-start | bytes 786440 | tf_op jit(solution)/shard_map/ppermute | solution.py:50
  26.3 57.1 %copy-start.7 = (f32[512,512]{1,0:T(8,128)}, f32[512,512]{1,0:T(8,128)S(1)}, u32[]{:S(2)}) copy-start(f32[512,512]{1,0:T(8,128)S(1)} %convolution_multiply_fusion.3) | copy-start | bytes 3145732
  26.3 22.9 %collective-permute-start.3 = (f32[512,512]{1,0:T(8,128)S(1)}, f32[512,512]{1,0:T(8,128)}, u32[]{:S(2)}, u32[]{:S(2)}) collective-permute-start(f32[512,512]{1,0:T(8,128)S(1)} %convolution_multiply_fusion.3), channel_id=1, source_target_pairs={{0,1},{1,2},{2,3},{3,4},{4,5},{5,6},{6,7},{7,8},{8,9},{9,10},{10,1... | collective-permute-start | bytes 3145736 | tf_op jit(solution)/shard_map/ppermute | solution.py:35
  52.3 39.5 %copy-start.1 = (f32[512,512]{1,0:T(8,128)}, f32[512,512]{1,0:T(8,128)S(1)}, u32[]{:S(2)}) copy-start(f32[512,512]{1,0:T(8,128)S(1)} %convolution_select_fusion.13) | copy-start | bytes 3145732
  52.3 28.0 %collective-permute-start.4 = (f32[512,512]{1,0:T(8,128)S(1)}, f32[512,512]{1,0:T(8,128)}, u32[]{:S(2)}, u32[]{:S(2)}) collective-permute-start(f32[512,512]{1,0:T(8,128)S(1)} %convolution_select_fusion.13), channel_id=1, source_target_pairs={{0,2},{1,3},{2,4},{3,5},{4,6},{5,7},{6,8},{7,9},{8,10},{9,11},{10,... | collective-permute-start | bytes 3145736 | tf_op jit(solution)/shard_map/ppermute | solution.py:35
  83.4 16.7 %copy-start.3 = (f32[512,512]{1,0:T(8,128)}, f32[512,512]{1,0:T(8,128)S(1)}, u32[]{:S(2)}) copy-start(f32[512,512]{1,0:T(8,128)S(1)} %convolution_select_fusion.12) | copy-start | bytes 3145732
  83.4 16.7 %collective-permute-start.5 = (f32[512,512]{1,0:T(8,128)S(1)}, f32[512,512]{1,0:T(8,128)S(1)}, u32[]{:S(2)}, u32[]{:S(2)}) collective-permute-start(f32[512,512]{1,0:T(8,128)S(1)} %convolution_select_fusion.12), channel_id=1, source_target_pairs={{0,4},{1,5},{2,6},{3,7},{4,8},{5,9},{6,10},{7,11},{8,12},{9,13},{1... | collective-permute-start | bytes 3145736 | tf_op jit(solution)/shard_map/ppermute | solution.py:35
  96.9 27.1 %collective-permute-start.21 = (f32[512,512]{1,0:T(8,128)S(1)}, f32[512,512]{1,0:T(8,128)}, u32[]{:S(2)}, u32[]{:S(2)}) collective-permute-start(f32[512,512]{1,0:T(8,128)S(1)} %fusion.5), channel_id=1, source_target_pairs={{1,0},{2,1},{3,2},{4,3},{5,4},{6,5},{7,6},{8,7},{9,8},{10,9},{11,1... | collective-permute-start | bytes 3145736 | tf_op jit(solution)/shard_map/ppermute | solution.py:35
  103.0 30.7 %collective-permute-start.6 = (f32[512,512]{1,0:T(8,128)}, f32[512,512]{1,0:T(8,128)}, u32[]{:S(2)}, u32[]{:S(2)}) collective-permute-start(f32[512,512]{1,0:T(8,128)} %convolution_select_fusion.11), channel_id=1, source_target_pairs={{0,8},{1,9},{2,10},{3,11},{4,12},{5,13},{6,14},{7,15},{8,16},{9,17... | collective-permute-start | bytes 3145736 | tf_op jit(solution)/shard_map/ppermute | solution.py:35
  127.1 27.7 %collective-permute-start.23 = (f32[512,512]{1,0:T(8,128)S(1)}, f32[512,512]{1,0:T(8,128)S(1)}, u32[]{:S(2)}, u32[]{:S(2)}) collective-permute-start(f32[512,512]{1,0:T(8,128)S(1)} %convolution_select_fusion.6), channel_id=1, source_target_pairs={{2,0},{3,1},{4,2},{5,3},{6,4},{7,5},{8,6},{9,7},{10,8},{11,9},{12,... | collective-permute-start | bytes 3145736 | tf_op jit(solution)/shard_map/ppermute | solution.py:35
  137.4 51.9 %copy-start.4 = (f32[512,512]{1,0:T(8,128)}, f32[512,512]{1,0:T(8,128)S(1)}, u32[]{:S(2)}) copy-start(f32[512,512]{1,0:T(8,128)S(1)} %convolution_select_fusion.10) | copy-start | bytes 3145732
  137.4 51.9 %collective-permute-start.7 = (f32[512,512]{1,0:T(8,128)S(1)}, f32[512,512]{1,0:T(8,128)S(1)}, u32[]{:S(2)}, u32[]{:S(2)}) collective-permute-start(f32[512,512]{1,0:T(8,128)S(1)} %convolution_select_fusion.10), channel_id=1, source_target_pairs={{0,16},{1,17},{2,18},{3,19},{4,20},{5,21},{6,22},{7,23},{8,24},{9,... | collective-permute-start | bytes 3145736 | tf_op jit(solution)/shard_map/ppermute | solution.py:35
  140.3 46.1 %copy-start.8 = (f32[512,512]{1,0:T(8,128)S(1)}, f32[512,512]{1,0:T(8,128)}, u32[]{:S(2)}) copy-start(f32[512,512]{1,0:T(8,128)} %copy-done.7) | copy-start | bytes 3145732
  141.3 45.1 %collective-permute-start.10 = (f32[4,512]{1,0:T(4,128)S(1)}, f32[4,512]{1,0:T(4,128)S(1)}, u32[]{:S(2)}, u32[]{:S(2)}) collective-permute-start(f32[4,512]{1,0:T(4,128)S(1)} %fusion.46), channel_id=1, source_target_pairs={{0,1},{1,2},{2,3},{3,4},{4,5},{5,6},{6,7},{7,8},{8,9},{9,10},{10,1... | collective-permute-start | bytes 24584 | tf_op jit(solution)/shard_map/ppermute | solution.py:35
  157.7 41.3 %copy-start.2 = (f32[512,512]{1,0:T(8,128)S(1)}, f32[512,512]{1,0:T(8,128)}, u32[]{:S(2)}) copy-start(f32[512,512]{1,0:T(8,128)} %copy-done.1) | copy-start | bytes 3145732
  157.7 68.8 %collective-permute-start.25 = (f32[512,512]{1,0:T(8,128)}, f32[512,512]{1,0:T(8,128)}, u32[]{:S(2)}, u32[]{:S(2)}) collective-permute-start(f32[512,512]{1,0:T(8,128)} %convolution_select_fusion.5), channel_id=1, source_target_pairs={{4,0},{5,1},{6,2},{7,3},{8,4},{9,5},{10,6},{11,7},{12,8},{13,9},{1... | collective-permute-start | bytes 3145736 | tf_op jit(solution)/shard_map/ppermute | solution.py:35
  187.4 11.6 %collective-permute-start.11 = (f32[4,512]{1,0:T(4,128)S(1)}, f32[4,512]{1,0:T(4,128)S(1)}, u32[]{:S(2)}, u32[]{:S(2)}) collective-permute-start(f32[4,512]{1,0:T(4,128)S(1)} %fusion.45), channel_id=1, source_target_pairs={{0,2},{1,3},{2,4},{3,5},{4,6},{5,7},{6,8},{7,9},{8,10},{9,11},{10,... | collective-permute-start | bytes 24584 | tf_op jit(solution)/shard_map/ppermute | solution.py:35
  192.2 70.3 %collective-permute-start.8 = (f32[512,512]{1,0:T(8,128)}, f32[512,512]{1,0:T(8,128)}, u32[]{:S(2)}, u32[]{:S(2)}) collective-permute-start(f32[512,512]{1,0:T(8,128)} %convolution_select_fusion.9), channel_id=1, source_target_pairs={{0,32},{1,33},{2,34},{3,35},{4,36},{5,37},{6,38},{7,39},{8,40},{9,... | collective-permute-start | bytes 3145736 | tf_op jit(solution)/shard_map/ppermute | solution.py:35
  199.9 22.5 %collective-permute-start.12 = (f32[4,512]{1,0:T(4,128)S(1)}, f32[4,512]{1,0:T(4,128)S(1)}, u32[]{:S(2)}, u32[]{:S(2)}) collective-permute-start(f32[4,512]{1,0:T(4,128)S(1)} %fusion.44), channel_id=1, source_target_pairs={{0,4},{1,5},{2,6},{3,7},{4,8},{5,9},{6,10},{7,11},{8,12},{9,13},{1... | collective-permute-start | bytes 24584 | tf_op jit(solution)/shard_map/ppermute | solution.py:35
  224.6 18.6 %collective-permute-start.13 = (f32[4,512]{1,0:T(4,128)S(1)}, f32[4,512]{1,0:T(4,128)S(1)}, u32[]{:S(2)}, u32[]{:S(2)}) collective-permute-start(f32[4,512]{1,0:T(4,128)S(1)} %fusion.43), channel_id=1, source_target_pairs={{0,8},{1,9},{2,10},{3,11},{4,12},{5,13},{6,14},{7,15},{8,16},{9,17... | collective-permute-start | bytes 24584 | tf_op jit(solution)/shard_map/ppermute | solution.py:35
  231.2 37.9 %copy-start.5 = (f32[512,512]{1,0:T(8,128)S(1)}, f32[512,512]{1,0:T(8,128)}, u32[]{:S(2)}) copy-start(f32[512,512]{1,0:T(8,128)} %copy-done.4) | copy-start | bytes 3145732
  231.2 52.4 %collective-permute-start.27 = (f32[512,512]{1,0:T(8,128)}, f32[512,512]{1,0:T(8,128)}, u32[]{:S(2)}, u32[]{:S(2)}) collective-permute-start(f32[512,512]{1,0:T(8,128)} %convolution_select_fusion.4), channel_id=1, source_target_pairs={{8,0},{9,1},{10,2},{11,3},{12,4},{13,5},{14,6},{15,7},{16,8},{17,9... | collective-permute-start | bytes 3145736 | tf_op jit(solution)/shard_map/ppermute | solution.py:35
  245.4 23.7 %collective-permute-start.14 = (f32[4,512]{1,0:T(4,128)S(1)}, f32[4,512]{1,0:T(4,128)S(1)}, u32[]{:S(2)}, u32[]{:S(2)}) collective-permute-start(f32[4,512]{1,0:T(4,128)S(1)} %fusion.42), channel_id=1, source_target_pairs={{0,16},{1,17},{2,18},{3,19},{4,20},{5,21},{6,22},{7,23},{8,24},{9,... | collective-permute-start | bytes 24584 | tf_op jit(solution)/shard_map/ppermute | solution.py:35
  267.2 28.5 %collective-permute-start.9 = (f32[512,512]{1,0:T(8,128)}, f32[512,512]{1,0:T(8,128)}, u32[]{:S(2)}, u32[]{:S(2)}) collective-permute-start(f32[512,512]{1,0:T(8,128)} %convolution_select_fusion.8), channel_id=1, source_target_pairs={{0,64},{1,65},{2,66},{3,67},{4,68},{5,69},{6,70},{7,71},{8,72},{9,... | collective-permute-start | bytes 3145736 | tf_op jit(solution)/shard_map/ppermute | solution.py:35
  270.1 9.5 %collective-permute-start.15 = (f32[4,512]{1,0:T(4,128)S(1)}, f32[4,512]{1,0:T(4,128)S(1)}, u32[]{:S(2)}, u32[]{:S(2)}) collective-permute-start(f32[4,512]{1,0:T(4,128)S(1)} %fusion.41), channel_id=1, source_target_pairs={{0,32},{1,33},{2,34},{3,35},{4,36},{5,37},{6,38},{7,39},{8,40},{9,... | collective-permute-start | bytes 24584 | tf_op jit(solution)/shard_map/ppermute | solution.py:35
  281.7 11.7 %collective-permute-start.16 = (f32[4,512]{1,0:T(4,128)S(1)}, f32[4,512]{1,0:T(4,128)S(1)}, u32[]{:S(2)}, u32[]{:S(2)}) collective-permute-start(f32[4,512]{1,0:T(4,128)S(1)} %fusion.40), channel_id=1, source_target_pairs={{0,64},{1,65},{2,66},{3,67},{4,68},{5,69},{6,70},{7,71},{8,72},{9,... | collective-permute-start | bytes 24584 | tf_op jit(solution)/shard_map/ppermute | solution.py:35
  288.3 12.1 %copy-start.10 = (f32[4,512]{1,0:T(4,128)S(1)}, f32[4,512]{1,0:T(4,128)}, u32[]{:S(2)}) copy-start(f32[4,512]{1,0:T(4,128)} %param.8) | copy-start | bytes 24580
  288.3 50.4 %collective-permute-start.29 = (f32[512,512]{1,0:T(8,128)}, f32[512,512]{1,0:T(8,128)}, u32[]{:S(2)}, u32[]{:S(2)}) collective-permute-start(f32[512,512]{1,0:T(8,128)} %convolution_select_fusion.3), channel_id=1, source_target_pairs={{16,0},{17,1},{18,2},{19,3},{20,4},{21,5},{22,6},{23,7},{24,8},{25... | collective-permute-start | bytes 3145736 | tf_op jit(solution)/shard_map/ppermute | solution.py:35
  299.4 1.0 copy-start.6
  301.4 2.7 collective-permute-start.17
  306.2 39.2 %collective-permute-start.18 = (f32[4,512]{1,0:T(4,128)S(1)}, f32[4,512]{1,0:T(4,128)S(1)}, u32[]{:S(2)}, u32[]{:S(2)}) collective-permute-start(f32[4,512]{1,0:T(4,128)S(1)} %fusion.38), channel_id=1, source_target_pairs={{0,1},{1,2},{2,3},{3,4},{4,5},{5,6},{6,7},{7,8},{8,9},{9,10},{10,1... | collective-permute-start | bytes 24584 | tf_op jit(solution)/shard_map/ppermute | solution.py:35
  343.5 52.3 %collective-permute-start.31 = (f32[512,512]{1,0:T(8,128)}, f32[512,512]{1,0:T(8,128)}, u32[]{:S(2)}, u32[]{:S(2)}) collective-permute-start(f32[512,512]{1,0:T(8,128)} %convolution_select_fusion.2), channel_id=1, source_target_pairs={{32,0},{33,1},{34,2},{35,3},{36,4},{37,5},{38,6},{39,7},{40,8},{41... | collective-permute-start | bytes 3145736 | tf_op jit(solution)/shard_map/ppermute | solution.py:35
  356.0 22.6 %collective-permute-start.19 = (f32[4,512]{1,0:T(4,128)S(1)}, f32[4,512]{1,0:T(4,128)S(1)}, u32[]{:S(2)}, u32[]{:S(2)}) collective-permute-start(f32[4,512]{1,0:T(4,128)S(1)} %fusion.26), channel_id=1, source_target_pairs={{1,0},{2,1},{3,2},{4,3},{5,4},{6,5},{7,6},{8,7},{9,8},{10,9},{11,1... | collective-permute-start | bytes 24584 | tf_op jit(solution)/shard_map/ppermute | solution.py:35
  379.6 11.0 %collective-permute-start.20 = (f32[4,512]{1,0:T(4,128)S(1)}, f32[4,512]{1,0:T(4,128)S(1)}, u32[]{:S(2)}, u32[]{:S(2)}) collective-permute-start(f32[4,512]{1,0:T(4,128)S(1)} %fusion.24), channel_id=1, source_target_pairs={{2,0},{3,1},{4,2},{5,3},{6,4},{7,5},{8,6},{9,7},{10,8},{11,9},{12,... | collective-permute-start | bytes 24584 | tf_op jit(solution)/shard_map/ppermute | solution.py:35
  391.5 10.0 %collective-permute-start.22 = (f32[4,512]{1,0:T(4,128)S(1)}, f32[4,512]{1,0:T(4,128)S(1)}, u32[]{:S(2)}, u32[]{:S(2)}) collective-permute-start(f32[4,512]{1,0:T(4,128)S(1)} %fusion.23), channel_id=1, source_target_pairs={{4,0},{5,1},{6,2},{7,3},{8,4},{9,5},{10,6},{11,7},{12,8},{13,9},{1... | collective-permute-start | bytes 24584 | tf_op jit(solution)/shard_map/ppermute | solution.py:35
  399.5 56.5 %collective-permute-start.33 = (f32[512,512]{1,0:T(8,128)S(1)}, f32[512,512]{1,0:T(8,128)S(1)}, u32[]{:S(2)}, u32[]{:S(2)}) collective-permute-start(f32[512,512]{1,0:T(8,128)S(1)} %convolution_select_fusion.1), channel_id=1, source_target_pairs={{64,0},{65,1},{66,2},{67,3},{68,4},{69,5},{70,6},{71,7},{72,8},{73... | collective-permute-start | bytes 3145736 | tf_op jit(solution)/shard_map/ppermute | solution.py:35
  403.7 19.1 %collective-permute-start.24 = (f32[4,512]{1,0:T(4,128)S(1)}, f32[4,512]{1,0:T(4,128)S(1)}, u32[]{:S(2)}, u32[]{:S(2)}) collective-permute-start(f32[4,512]{1,0:T(4,128)S(1)} %fusion.22), channel_id=1, source_target_pairs={{8,0},{9,1},{10,2},{11,3},{12,4},{13,5},{14,6},{15,7},{16,8},{17,9... | collective-permute-start | bytes 24584 | tf_op jit(solution)/shard_map/ppermute | solution.py:35
  425.0 8.6 %collective-permute-start.26 = (f32[4,512]{1,0:T(4,128)S(1)}, f32[4,512]{1,0:T(4,128)S(1)}, u32[]{:S(2)}, u32[]{:S(2)}) collective-permute-start(f32[4,512]{1,0:T(4,128)S(1)} %fusion.21), channel_id=1, source_target_pairs={{16,0},{17,1},{18,2},{19,3},{20,4},{21,5},{22,6},{23,7},{24,8},{25... | collective-permute-start | bytes 24584 | tf_op jit(solution)/shard_map/ppermute | solution.py:35
  435.7 10.4 %collective-permute-start.28 = (f32[4,512]{1,0:T(4,128)S(1)}, f32[4,512]{1,0:T(4,128)S(1)}, u32[]{:S(2)}, u32[]{:S(2)}) collective-permute-start(f32[4,512]{1,0:T(4,128)S(1)} %fusion.20), channel_id=1, source_target_pairs={{32,0},{33,1},{34,2},{35,3},{36,4},{37,5},{38,6},{39,7},{40,8},{41... | collective-permute-start | bytes 24584 | tf_op jit(solution)/shard_map/ppermute | solution.py:35
  448.2 5.5 %collective-permute-start.30 = (f32[4,512]{1,0:T(4,128)S(1)}, f32[4,512]{1,0:T(4,128)S(1)}, u32[]{:S(2)}, u32[]{:S(2)}) collective-permute-start(f32[4,512]{1,0:T(4,128)S(1)} %fusion.19), channel_id=1, source_target_pairs={{64,0},{65,1},{66,2},{67,3},{68,4},{69,5},{70,6},{71,7},{72,8},{73... | collective-permute-start | bytes 24584 | tf_op jit(solution)/shard_map/ppermute | solution.py:35
  454.8 7.1 %collective-permute-start.32 = (f32[4,512]{1,0:T(4,128)S(1)}, f32[4,512]{1,0:T(4,128)S(1)}, u32[]{:S(2)}, u32[]{:S(2)}) collective-permute-start(f32[4,512]{1,0:T(4,128)S(1)} %fusion.18), channel_id=1, source_target_pairs={{128,0},{129,1},{130,2},{131,3},{132,4},{133,5},{134,6},{135,7},{1... | collective-permute-start | bytes 24584 | tf_op jit(solution)/shard_map/ppermute | solution.py:35
  462.8 5.5 %collective-permute-start.34 = (f32[4,512]{1,0:T(4,128)S(1)}, f32[4,512]{1,0:T(4,128)S(1)}, u32[]{:S(2)}, u32[]{:S(2)}) collective-permute-start(f32[4,512]{1,0:T(4,128)S(1)} %fusion.17), channel_id=1, source_target_pairs={{1,0},{2,1},{3,2},{4,3},{5,4},{6,5},{7,6},{8,7},{9,8},{10,9},{11,1... | collective-permute-start | bytes 24584 | tf_op jit(solution)/shard_map/ppermute | solution.py:35
